TPU v7x, 32 devices: a whole 2x2x4 slice. The times are simulated.
32 devices in a mesh: dp: 8 (over y, x, core), fsdp: 4 (over z).
Axes of the slice: x: 2, y: 2, z: 4, core: 2. Of those that a mesh axis runs over, the one named last changes fastest.
Arguments:
- query_cache: bfloat16 [384, 1024], P('dp', 'fsdp'), may hold values from -8 to 8
- region_cache: bfloat16 [384, 1024], P('dp', 'fsdp'), may hold values from -8 to 8
- positive: int32 [384], P('dp'), may hold values from 0 to 383, each once
- hidden_states: bfloat16 [4096, 4096], P(('dp', 'fsdp')), may hold values from -12 to 12
- segment_ids: int32 [8, 512], P('dp', 'fsdp'), may hold values from 0 to 47, never falling along the last dimension, each value on 1 to 21 neighbouring positions
- norm_gain: bfloat16 [4096], replicated, may hold values from 0.099609375 to 1.8984375
- proj_weight: bfloat16 [4096, 1024], P('fsdp'), may hold values from -1 to 1
Outputs:
- mean_loss: float32 [], replicated
- query_grad: float32 [384, 1024], P('dp', 'fsdp')
- region_grad: float32 [384, 1024], P('dp', 'fsdp')
- hidden_grad: bfloat16 [4096, 4096], P(('dp', 'fsdp'))
- gain_grad: float32 [4096], replicated
- proj_grad: float32 [4096, 1024], P('dp', 'fsdp')
Inputs may be any that keep to these rules, and one draw needn't show every extreme that they name: Each region is the positive of exactly one instruction. `segment_ids`: within a pair group the ids never fall, every instruction has at least one token, and one has exactly 21.
All inputs are finite; a program needn't handle non-finite values.
Results may differ from a plain program's by a relative error of at most 0.0088.
Values may be sent and summed in bfloat16 or wider, within the bound.
No kernel may reach another device: no remote copies, remote signals or barrier semaphores. Data moves between devices by JAX's collectives and lax.ppermute only.
A program may use at most 64 MiB of HBM per device.

v0:
```python
import jax
import jax.numpy as jnp
from jax import lax
from jax.sharding import PartitionSpec as P

E = 1024
EPS = 1e-05


def local(query_cache, region_cache, positive, hidden_states, segment_ids, norm_gain, proj_weight):
    row_count = query_cache.shape[0]
    data_count = lax.axis_size("dp")
    pair_count = row_count * data_count
    logit_scale = float(E) ** (-0.5)
    contract_last = (((1,), (1,)), ((), ()))
    contract_first = (((0,), (0,)), ((), ()))
    region_all, query_all = (
        lax.all_gather(region_cache, "dp", axis=0, tiled=True),
        lax.all_gather(query_cache, "dp", axis=0, tiled=True),
    )
    partial_value = lax.dot_general(
        query_cache, region_all, contract_last, preferred_element_type=jnp.float32
    )
    scores = lax.psum(partial_value, "fsdp") * logit_scale
    row_max = jnp.max(scores, axis=1, keepdims=True)
    log_total = row_max[:, 0] + jnp.log(jnp.sum(jnp.exp(scores - row_max), axis=1))
    columns = lax.broadcasted_iota(jnp.int32, (1, pair_count), 1)
    matched = columns == positive[:, None]
    target_score = jnp.sum(jnp.where(matched, scores, jnp.zeros_like(scores)), axis=1)
    loss_local = jnp.sum(log_total - target_score)
    grad_probs = (jnp.exp(scores - log_total[:, None]) - matched.astype(jnp.float32)).astype(
        jnp.bfloat16
    )
    query_grad = logit_scale * jnp.dot(grad_probs, region_all, preferred_element_type=jnp.float32)
    totals_all, targets_all = (
        lax.all_gather(log_total, "dp", axis=0, tiled=True),
        lax.all_gather(positive.astype(jnp.float32), "dp", axis=0, tiled=True),
    )
    partial_t = lax.dot_general(
        region_cache, query_all, contract_last, preferred_element_type=jnp.float32
    )
    scores_t = lax.psum(partial_t, "fsdp") * logit_scale
    own_rows = (
        lax.axis_index("dp") * row_count + lax.broadcasted_iota(jnp.int32, (row_count, 1), 0)
    ).astype(jnp.float32)
    matched_t = targets_all[None, :] == own_rows
    probs_t = (jnp.exp(scores_t - totals_all[None, :]) - matched_t.astype(jnp.float32)).astype(
        jnp.bfloat16
    )
    region_grad = logit_scale * jnp.dot(probs_t, query_all, preferred_element_type=jnp.float32)
    gain = norm_gain.astype(jnp.float32)
    states = hidden_states.astype(jnp.float32)
    inv_rms = lax.rsqrt(jnp.mean(states * states, axis=1, keepdims=True) + EPS)
    normed = (states * inv_rms * gain).astype(jnp.bfloat16)
    labels = lax.broadcasted_iota(jnp.int32, (row_count, 1), 0)
    member = segment_ids[0][None, :] == labels
    pooled_part = jnp.dot(member.astype(jnp.bfloat16), normed, preferred_element_type=jnp.float32)
    counts_part = jnp.sum(member.astype(jnp.float32), axis=1)
    pooled, counts = lax.psum((pooled_part, counts_part), "fsdp")
    mean_pooled = (pooled / counts[:, None]).astype(jnp.bfloat16)
    grad_low = query_grad.astype(jnp.bfloat16)
    grad_full = lax.all_gather(grad_low, "fsdp", axis=1, tiled=True)
    mean_part = lax.dot_general(
        grad_full, proj_weight, contract_last, preferred_element_type=jnp.float32
    )
    mean_grad = lax.all_gather(mean_part, "fsdp", axis=1, tiled=True)
    pool_grad = mean_grad / counts[:, None]
    normed_grad = lax.dot_general(
        member.astype(jnp.float32),
        pool_grad,
        contract_first,
        precision=lax.Precision.HIGHEST,
        preferred_element_type=jnp.float32,
    )
    gain_part = jnp.sum(normed_grad * states * inv_rms, axis=0)
    scaled = gain * normed_grad
    inner = jnp.mean(scaled * states, axis=1, keepdims=True)
    hidden_grad = (inv_rms * scaled - states * inv_rms**3 * inner).astype(jnp.bfloat16)
    proj_grad = lax.psum_scatter(
        lax.dot_general(mean_pooled, grad_low, contract_first, preferred_element_type=jnp.float32),
        "dp",
        scatter_dimension=0,
        tiled=True,
    )
    loss_total = lax.psum(loss_local, "dp")
    gain_grad = lax.psum(gain_part, ("dp", "fsdp"))
    mean_loss = loss_total / pair_count
    return (mean_loss, query_grad, region_grad, hidden_grad, gain_grad, proj_grad)


def solution(mesh):
    in_specs = (
        P("dp", "fsdp"),
        P("dp", "fsdp"),
        P("dp"),
        P(("dp", "fsdp"), None),
        P("dp", "fsdp"),
        P(),
        P("fsdp", None),
    )
    out_specs = (
        P(),
        P("dp", "fsdp"),
        P("dp", "fsdp"),
        P(("dp", "fsdp"), None),
        P(),
        P("dp", "fsdp"),
    )
    return jax.shard_map(local, mesh=mesh, in_specs=in_specs, out_specs=out_specs, check_vma=False)
```

profile of v0, /device:TPU:12, one launch (start us, length us, event | category | flops | bytes accessed | tf_op | source)
XLA Modules:
  0.0 194.4 jit_solution(16001850921238040908)
XLA Ops:
  7.2 1.7 fusion
  8.9 0.6 multiply_multiply_fusion
  9.5 0.7 convert_element_type.53
  10.2 9.2 %all_gather.19 = bf16[384,256]{1,0:T(8,128)(2,1)S(1)} all-gather(bf16[48,256]{1,0:T(8,128)(2,1)} %param.7), channel_id=1, replica_groups=mesh['dp'=8,'fsdp'=4] {'dp'}, dimensions={0}, use_global_device_ids=true | all-gather | bytes 221184 | tf_op jit(solution)/shard_map/all_gather | solution.py:19
  19.5 8.5 %all_gather.18 = bf16[384,256]{1,0:T(8,128)(2,1)S(1)} all-gather(bf16[48,256]{1,0:T(8,128)(2,1)} %param.8), channel_id=1, replica_groups=mesh['dp'=8,'fsdp'=4] {'dp'}, dimensions={0}, use_global_device_ids=true | all-gather | bytes 221184 | tf_op jit(solution)/shard_map/all_gather | solution.py:18
  27.9 1.6 fusion.32
  29.5 1.6 fusion.31
  31.1 1.4 fusion.9
  32.5 1.2 dynamic-slice
  34.4 1.3 convert_reduce_fusion
  35.7 9.7 %psum.45 = f32[48]{0:T(128)} all-reduce(f32[48]{0:T(128)} %convert_reduce_fusion), channel_id=1, replica_groups=mesh['dp'=8,'fsdp'=4] {'fsdp'}, use_global_device_ids=true, to_apply=%region_9.10 | all-reduce | flops 48 | bytes 384 | tf_op jit(solution)/shard_map/psum | solution.py:59
  45.4 37.4 %all-reduce.6.cloned.1.call-done = (f32[48,384]{1,0:T(8,128)}, f32[48,384]{1,0:T(8,128)}, f32[48,4096]{1,0:T(8,128)}) async-done(((f32[48,384]{1,0:T(8,128)}, f32[48,384]{1,0:T(8,128)}, f32[48,4096]{1,0:T(8,128)}), (f32[48,384]{1,0:T(8,128)}, f32[48,384]{1,0:T(8,128)}, f32[48,4096]{1,0:T(8,128)})) %all-reduce.6.cloned.1.call-update) | async-done | bytes 933904 | tf_op jit(solution)/shard_map/psum | solution.py:24
  82.8 1.0 multiply_reduce_fusion
  83.8 1.6 select_reduce_fusion
  85.5 1.7 fusion.30
  87.9 3.9 %fusion.15 = f32[4096,256]{1,0:T(8,128)} fusion(bf16[48,256]{1,0:T(8,128)(2,1)S(1)} %get-tuple-element.20, f32[48,4096]{1,0:T(8,128)} %get-tuple-element.15, f32[48]{0:T(128)} %psum.45), kind=kOutput, calls=%fused_computation.22 | convolution fusion | flops 101056512 | bytes 5005504 | tf_op jit(solution)/shard_map/dot_general | solution.py:80
  93.1 13.3 %all-reduce.2 = (f32[]{:T(128)}, f32[384]{0:T(512)S(1)}, f32[384]{0:T(512)S(1)}) all-reduce(f32[]{:T(128)} %subtract_reduce_fusion, f32[384]{0:T(512)S(1)} %convert_dynamic-update-slice_fusion, f32[384]{0:T(512)S(1)} %copy-done.6), channel_id=1, replica_groups=mesh['dp'=8,'fsdp'=4] {'dp'}, use_global_device_ids=true, to_apply=%region_5.6 | all-reduce | flops 769 | bytes 6152 | tf_op jit(solution)/shard_map/psum | solution.py:85
  107.1 12.2 %all_gather.22 = bf16[48,1024]{1,0:T(8,128)(2,1)S(1)} all-gather(bf16[48,256]{1,0:T(8,128)(2,1)S(1)} %copy-done.3), channel_id=1, replica_groups=mesh['dp'=8,'fsdp'=4] {'fsdp'}, dimensions={1}, use_global_device_ids=true | all-gather | bytes 122880 | tf_op jit(solution)/shard_map/all_gather | solution.py:62
  119.3 0.7 fusion.33
  120.0 17.5 %all_gather.23 = f32[48,4096]{1,0:T(8,128)S(1)} all-gather(f32[48,1024]{1,0:T(8,128)S(1)} %fusion.33), channel_id=1, replica_groups=mesh['dp'=8,'fsdp'=4] {'fsdp'}, dimensions={1}, use_global_device_ids=true | all-gather | bytes 983040 | tf_op jit(solution)/shard_map/all_gather | solution.py:66
  137.6 2.8 %fusion.6 = (f32[4096]{0:T(1024)S(1)}, f32[128]{0:T(128)S(1)}, f32[128,4096]{1,0:T(8,128)}) fusion(bf16[128,4096]{1,0:T(8,128)(2,1)S(1)} %copy-done.1, f32[128]{0:T(128)S(1)} %copy-done.12, f32[4096]{0:T(1024)S(1)} %convert_element_type.53, f32[48,4096]{1,0:T(8,128)S(1)} %all_gather.23, f32[48]{0:T(128)S(1)} %copy-done.13, s32[128]{0:T(128)S(1)} %bitcast.13), kind=kOutput, calls=%fused_computation.11 | convolution fusion | flops 305858432 | bytes 3966656 | tf_op jit(solution)/shard_map/dot_general | solution.py:68
  140.4 42.0 %psum.46 = f32[4096]{0:T(1024)} all-reduce(f32[4096]{0:T(1024)S(1)} %get-tuple-element.6), channel_id=1, replica_groups=mesh['dp'=8,'fsdp'=4] {'dp','fsdp'}, use_global_device_ids=true, to_apply=%region_12.13 | all-reduce | flops 4096 | bytes 32768 | tf_op jit(solution)/shard_map/psum | solution.py:86
  182.5 0.8 convolution_multiply_fusion
  183.3 3.2 %fusion.3 = bf16[128,4096]{1,0:T(8,128)(2,1)} fusion(bf16[128,4096]{1,0:T(8,128)(2,1)S(1)} %copy-done.1, f32[128,4096]{1,0:T(8,128)} %get-tuple-element.22, f32[128]{0:T(128)S(1)} %broadcast_multiply_fusion, f32[128]{0:T(128)S(1)} %copy-done.10, f32[4096]{0:T(1024)S(1)} %convert_element_type.53, f32[128]{0:T(128)S(1)} %copy-done.12), kind=kLoop, calls=%fused_computation.8 | loop fusion | flops 3670016 | bytes 4212224 | tf_op jit(solution)/shard_map/convert_element_type | solution.py:78
  (46 shorter events, 2.1 us)
Async XLA Ops:
  7.2 112.1 %copy-start = (bf16[1024,1024]{1,0:T(8,128)(2,1)S(1)}, bf16[1024,1024]{1,0:T(8,128)(2,1)}, u32[]{:S(2)}) copy-start(bf16[1024,1024]{1,0:T(8,128)(2,1)} %param.13) | copy-start | bytes 6291460
  7.2 23.9 %copy-start.1 = (bf16[128,4096]{1,0:T(8,128)(2,1)S(1)}, bf16[128,4096]{1,0:T(8,128)(2,1)}, u32[]{:S(2)}) copy-start(bf16[128,4096]{1,0:T(8,128)(2,1)} %param.10) | copy-start | bytes 3145732
  7.2 75.6 %all-reduce.6.cloned.1.call-start = ((), (), s32[]{:S(2)}) async-start(), calls=%async_computation.2 | async-start | bytes 1867776 | tf_op jit(solution)/shard_map/psum | solution.py:24
  7.2 23.8 %copy-start.15 = (s32[1,128]{1,0:T(1,128)S(1)}, s32[1,128]{1,0:T(1,128)}, u32[]{:S(2)}) copy-start(s32[1,128]{1,0:T(1,128)} %param.11) | copy-start | bytes 1540
  9.5 21.5 %copy-start.11 = (f32[128]{0:T(128)}, f32[128]{0:T(128)S(1)}, u32[]{:S(2)}) copy-start(f32[128]{0:T(128)S(1)} %get-tuple-element.19) | copy-start | bytes 1540
  32.4 154.0 %reduce-scatter.2.cloned.1.call-start = ((), (), s32[]{:S(2)}) async-start(), calls=%async_computation.1 | async-start | bytes 4718592 | tf_op jit(solution)/shard_map/reduce_scatter | solution.py:79
  85.5 1.7 copy-start.5
  85.5 1.7 copy-start.8
  87.2 0.6 copy-start.2
  91.7 0.7 copy-start.7
  91.7 0.7 copy-start.9
  91.8 0.7 copy-start.14
  91.8 1.3 copy-start.6
  91.8 15.3 %copy-start.3 = (bf16[48,256]{1,0:T(8,128)(2,1)S(1)}, bf16[48,256]{1,0:T(8,128)(2,1)}, u32[]{:S(2)}) copy-start(bf16[48,256]{1,0:T(8,128)(2,1)} %copy-done.2) | copy-start | bytes 73732
  91.8 45.8 %copy-start.12 = (f32[128]{0:T(128)S(1)}, f32[128]{0:T(128)}, u32[]{:S(2)}) copy-start(f32[128]{0:T(128)} %copy-done.11) | copy-start | bytes 1540
  91.8 45.8 %copy-start.13 = (f32[48]{0:T(128)S(1)}, f32[48]{0:T(128)}, u32[]{:S(2)}) copy-start(f32[48]{0:T(128)} %psum.45) | copy-start | bytes 580
  91.8 45.8 %copy-start.16 = (s32[1,128]{1,0:T(1,128)S(1)}, s32[1,128]{1,0:T(1,128)}, u32[]{:S(2)}) copy-start(s32[1,128]{1,0:T(1,128)} %param.11) | copy-start | bytes 1540
  137.6 44.9 %copy-start.4 = (f32[48,384]{1,0:T(8,128)S(1)}, f32[48,384]{1,0:T(8,128)}, u32[]{:S(2)}) copy-start(f32[48,384]{1,0:T(8,128)} %get-tuple-element.14) | copy-start | bytes 221188
  137.6 45.7 %copy-start.10 = (f32[128]{0:T(128)S(1)}, f32[128]{0:T(128)}, u32[]{:S(2)}) copy-start(f32[128]{0:T(128)} %get-tuple-element.18) | copy-start | bytes 1540
Sparse Core Ops, SparseCore 0:
  32.6 50.2 all-reduce.5
  91.9 50.7 reduce-scatter.1
where the time goes:
time: 195 us; the launch traced here: 194 us
  blocking collectives  113 us (58%)
  waiting for transfers between devices  37.4 us (19%)
  between operations  16.6 us (9%)
  matrix products  14.5 us (7%)
  other arithmetic  10.8 us (6%)
  local copies, waits for them, and re-layouts  2.47 us (1%)
    psum x1, blocking collectives, local(): gain_grad = lax.psum(gain_part, ('dp', 'fsdp'))  42 us
    psum x1, waiting for transfers between devices, local(): scores = lax.psum(partial_value, 'fsdp') * logit_scale  37.4 us
    all_gather x1, blocking collectives, local(): mean_grad = lax.all_gather(mean_part, 'fsdp', axis=1, tiled=True)  17.5 us
    psum x1, blocking collectives, local(): loss_total = lax.psum(loss_local, 'dp')  13.3 us
    all_gather x1, blocking collectives, local(): grad_full = lax.all_gather(grad_low, 'fsdp', axis=1, tiled=True)  12.2 us
    psum x1, blocking collectives, local(): pooled, counts = lax.psum((pooled_part, counts_part), 'fsdp')  9.73 us
    all_gather x1, blocking collectives, local(): lax.all_gather(query_cache, 'dp', axis=0, tiled=True)  9.23 us
    all_gather x1, blocking collectives, local(): lax.all_gather(region_cache, 'dp', axis=0, tiled=True)  8.47 us
  transfers between devices with their start and end apart: 2, of which 1 were waited for; matrix products, arithmetic and copies ran while one was open for 6% of the time, Pallas kernels for 0%

commit v1 on v0

--- a/solution.py
+++ b/solution.py
@@ -83,7 +83,7 @@
         tiled=True,
     )
     loss_total = lax.psum(loss_local, "dp")
-    gain_grad = lax.psum(gain_part, ("dp", "fsdp"))
+    gain_grad = jax.lax.all_gather(gain_part, ("dp", "fsdp")).sum(axis=0)
     mean_loss = loss_total / pair_count
     return (mean_loss, query_grad, region_grad, hidden_grad, gain_grad, proj_grad)
 

time: 195 us -> 234 us (1.20); the launches traced: 194 us -> 230 us
  blocking collectives: 113 us -> 145 us
    all_gather x0 -> x1, blocking collectives: none -> 74.1 us  [local(): gain_grad = jax.lax.all_gather(gain_part, ('dp', 'fsdp')).sum(axis=0)]
    psum x1 -> x0, blocking collectives: 42 us -> none  [local(): gain_grad = lax.psum(gain_part, ('dp', 'fsdp'))]
where the time goes in v1:
time: 234 us; the launch traced here: 230 us
  blocking collectives  145 us (62%)
  waiting for transfers between devices  37.4 us (16%)
  between operations  16.6 us (7%)
  matrix products  14.5 us (6%)
  other arithmetic  12.4 us (5%)
  local copies, waits for them, and re-layouts  4.4 us (2%)
    all_gather x1, blocking collectives, local(): gain_grad = jax.lax.all_gather(gain_part, ('dp', 'fsdp')).sum(axis=0)  74.1 us
    psum x1, waiting for transfers between devices, local(): scores = lax.psum(partial_value, 'fsdp') * logit_scale  37.4 us
    all_gather x1, blocking collectives, local(): mean_grad = lax.all_gather(mean_part, 'fsdp', axis=1, tiled=True)  17.5 us
    psum x1, blocking collectives, local(): loss_total = lax.psum(loss_local, 'dp')  13.3 us
    all_gather x1, blocking collectives, local(): grad_full = lax.all_gather(grad_low, 'fsdp', axis=1, tiled=True)  12.2 us
    psum x1, blocking collectives, local(): pooled, counts = lax.psum((pooled_part, counts_part), 'fsdp')  9.74 us
    all_gather x1, blocking collectives, local(): lax.all_gather(query_cache, 'dp', axis=0, tiled=True)  9.23 us
    all_gather x1, blocking collectives, local(): lax.all_gather(region_cache, 'dp', axis=0, tiled=True)  8.47 us
  transfers between devices with their start and end apart: 2, of which 1 were waited for; matrix products, arithmetic and copies ran while one was open for 6% of the time, Pallas kernels for 0%

profile of v1, /device:TPU:12, one launch (start us, length us, event | category | flops | bytes accessed | tf_op | source)
XLA Modules:
  0.0 230.0 jit_solution(14542525772632597278)
XLA Ops:
  7.2 1.7 fusion
  10.2 9.2 %all_gather.25 = bf16[384,256]{1,0:T(8,128)(2,1)S(1)} all-gather(bf16[48,256]{1,0:T(8,128)(2,1)} %param.7), channel_id=1, replica_groups=mesh['dp'=8,'fsdp'=4] {'dp'}, dimensions={0}, use_global_device_ids=true | all-gather | bytes 221184 | tf_op jit(solution)/shard_map/all_gather | solution.py:19
  19.4 8.5 %all_gather.24 = bf16[384,256]{1,0:T(8,128)(2,1)S(1)} all-gather(bf16[48,256]{1,0:T(8,128)(2,1)} %param.8), channel_id=1, replica_groups=mesh['dp'=8,'fsdp'=4] {'dp'}, dimensions={0}, use_global_device_ids=true | all-gather | bytes 221184 | tf_op jit(solution)/shard_map/all_gather | solution.py:18
  27.9 1.6 fusion.32
  29.4 1.6 fusion.31
  31.0 1.4 fusion.9
  32.4 1.2 dynamic-slice
  34.3 1.3 convert_reduce_fusion
  35.6 9.7 %psum.38 = f32[48]{0:T(128)} all-reduce(f32[48]{0:T(128)} %convert_reduce_fusion), channel_id=1, replica_groups=mesh['dp'=8,'fsdp'=4] {'fsdp'}, use_global_device_ids=true, to_apply=%region_9.10 | all-reduce | flops 48 | bytes 384 | tf_op jit(solution)/shard_map/psum | solution.py:59
  45.4 37.4 %all-reduce.6.cloned.1.call-done = (f32[48,384]{1,0:T(8,128)}, f32[48,384]{1,0:T(8,128)}, f32[48,4096]{1,0:T(8,128)}) async-done(((f32[48,384]{1,0:T(8,128)}, f32[48,384]{1,0:T(8,128)}, f32[48,4096]{1,0:T(8,128)}), (f32[48,384]{1,0:T(8,128)}, f32[48,384]{1,0:T(8,128)}, f32[48,4096]{1,0:T(8,128)})) %all-reduce.6.cloned.1.call-update) | async-done | bytes 933904 | tf_op jit(solution)/shard_map/psum | solution.py:24
  82.8 1.0 multiply_reduce_fusion
  83.7 1.6 select_reduce_fusion
  85.5 1.7 fusion.30
  87.8 3.9 %fusion.15 = f32[4096,256]{1,0:T(8,128)} fusion(bf16[48,256]{1,0:T(8,128)(2,1)S(1)} %get-tuple-element.20, f32[48,4096]{1,0:T(8,128)} %get-tuple-element.15, f32[48]{0:T(128)} %psum.38), kind=kOutput, calls=%fused_computation.22 | convolution fusion | flops 101056512 | bytes 5005504 | tf_op jit(solution)/shard_map/dot_general | solution.py:80
  93.0 13.3 %all-reduce.2 = (f32[]{:T(128)}, f32[384]{0:T(512)S(1)}, f32[384]{0:T(512)S(1)}) all-reduce(f32[]{:T(128)} %subtract_reduce_fusion, f32[384]{0:T(512)S(1)} %convert_dynamic-update-slice_fusion, f32[384]{0:T(512)S(1)} %copy-done.6), channel_id=1, replica_groups=mesh['dp'=8,'fsdp'=4] {'dp'}, use_global_device_ids=true, to_apply=%region_5.6 | all-reduce | flops 769 | bytes 6152 | tf_op jit(solution)/shard_map/psum | solution.py:85
  106.4 12.2 %all_gather.28 = bf16[48,1024]{1,0:T(8,128)(2,1)S(1)} all-gather(bf16[48,256]{1,0:T(8,128)(2,1)S(1)} %copy-done.3), channel_id=1, replica_groups=mesh['dp'=8,'fsdp'=4] {'fsdp'}, dimensions={1}, use_global_device_ids=true | all-gather | bytes 122880 | tf_op jit(solution)/shard_map/all_gather | solution.py:62
  118.5 0.7 fusion.33
  119.3 17.5 %all_gather.29 = f32[48,4096]{1,0:T(8,128)S(1)} all-gather(f32[48,1024]{1,0:T(8,128)S(1)} %fusion.33), channel_id=1, replica_groups=mesh['dp'=8,'fsdp'=4] {'fsdp'}, dimensions={1}, use_global_device_ids=true | all-gather | bytes 983040 | tf_op jit(solution)/shard_map/all_gather | solution.py:66
  136.8 2.8 %fusion.6 = (f32[4096]{0:T(1024)S(1)}, f32[128]{0:T(128)S(1)}, f32[128,4096]{1,0:T(8,128)}) fusion(bf16[128,4096]{1,0:T(8,128)(2,1)S(1)} %copy-done.1, f32[128]{0:T(128)S(1)} %copy-done.12, f32[4096]{0:T(1024)S(1)} %convert_element_type.53, f32[48,4096]{1,0:T(8,128)S(1)} %all_gather.29, f32[48]{0:T(128)S(1)} %copy-done.13, s32[128]{0:T(128)S(1)} %bitcast.13), kind=kOutput, calls=%fused_computation.11 | convolution fusion | flops 305858432 | bytes 3966656 | tf_op jit(solution)/shard_map/dot_general | solution.py:68
  139.7 74.1 %all-gather = f32[131072]{0:T(1024)} all-gather(f32[4096]{0:T(1024)S(1)} %get-tuple-element.6), channel_id=2, replica_groups=mesh['dp'=8,'fsdp'=4] {'dp','fsdp'}, dimensions={0}, use_global_device_ids=true | all-gather | bytes 540672 | tf_op jit(solution)/shard_map/all_gather | solution.py:86
  213.8 1.9 reshape.49
  216.4 1.7 reduce_sum.79
  218.1 0.8 convolution_multiply_fusion
  218.9 3.2 %fusion.3 = bf16[128,4096]{1,0:T(8,128)(2,1)} fusion(bf16[128,4096]{1,0:T(8,128)(2,1)S(1)} %copy-done.1, f32[128,4096]{1,0:T(8,128)} %get-tuple-element.22, f32[128]{0:T(128)S(1)} %broadcast_multiply_fusion, f32[128]{0:T(128)S(1)} %copy-done.10, f32[4096]{0:T(1024)S(1)} %convert_element_type.53, f32[128]{0:T(128)S(1)} %copy-done.12), kind=kLoop, calls=%fused_computation.8 | loop fusion | flops 3670016 | bytes 4212224 | tf_op jit(solution)/shard_map/convert_element_type | solution.py:78
  (48 shorter events, 3.4 us)
Async XLA Ops:
  7.2 111.4 %copy-start = (bf16[1024,1024]{1,0:T(8,128)(2,1)S(1)}, bf16[1024,1024]{1,0:T(8,128)(2,1)}, u32[]{:S(2)}) copy-start(bf16[1024,1024]{1,0:T(8,128)(2,1)} %param.13) | copy-start | bytes 6291460
  7.2 23.8 %copy-start.1 = (bf16[128,4096]{1,0:T(8,128)(2,1)S(1)}, bf16[128,4096]{1,0:T(8,128)(2,1)}, u32[]{:S(2)}) copy-start(bf16[128,4096]{1,0:T(8,128)(2,1)} %param.10) | copy-start | bytes 3145732
  7.2 75.6 %all-reduce.6.cloned.1.call-start = ((), (), s32[]{:S(2)}) async-start(), calls=%async_computation.2 | async-start | bytes 1867776 | tf_op jit(solution)/shard_map/psum | solution.py:24
  7.2 23.7 %copy-start.15 = (s32[1,128]{1,0:T(1,128)S(1)}, s32[1,128]{1,0:T(1,128)}, u32[]{:S(2)}) copy-start(s32[1,128]{1,0:T(1,128)} %param.11) | copy-start | bytes 1540
  9.5 21.5 %copy-start.11 = (f32[128]{0:T(128)}, f32[128]{0:T(128)S(1)}, u32[]{:S(2)}) copy-start(f32[128]{0:T(128)S(1)} %get-tuple-element.19) | copy-start | bytes 1540
  32.4 189.7 %reduce-scatter.2.cloned.1.call-start = ((), (), s32[]{:S(2)}) async-start(), calls=%async_computation.1 | async-start | bytes 4718592 | tf_op jit(solution)/shard_map/reduce_scatter | solution.py:79
  85.4 1.7 copy-start.5
  85.5 1.7 copy-start.8
  87.2 0.6 copy-start.2
  91.7 0.7 copy-start.7
  91.7 0.7 copy-start.9
  91.7 0.7 copy-start.14
  91.7 1.3 copy-start.6
  91.7 14.7 %copy-start.3 = (bf16[48,256]{1,0:T(8,128)(2,1)S(1)}, bf16[48,256]{1,0:T(8,128)(2,1)}, u32[]{:S(2)}) copy-start(bf16[48,256]{1,0:T(8,128)(2,1)} %copy-done.2) | copy-start | bytes 73732
  91.7 45.1 %copy-start.12 = (f32[128]{0:T(128)S(1)}, f32[128]{0:T(128)}, u32[]{:S(2)}) copy-start(f32[128]{0:T(128)} %copy-done.11) | copy-start | bytes 1540
  91.7 45.1 %copy-start.13 = (f32[48]{0:T(128)S(1)}, f32[48]{0:T(128)}, u32[]{:S(2)}) copy-start(f32[48]{0:T(128)} %psum.38) | copy-start | bytes 580
  91.7 45.1 %copy-start.16 = (s32[1,128]{1,0:T(1,128)S(1)}, s32[1,128]{1,0:T(1,128)}, u32[]{:S(2)}) copy-start(s32[1,128]{1,0:T(1,128)} %param.11) | copy-start | bytes 1540
  139.7 78.4 %copy-start.4 = (f32[48,384]{1,0:T(8,128)S(1)}, f32[48,384]{1,0:T(8,128)}, u32[]{:S(2)}) copy-start(f32[48,384]{1,0:T(8,128)} %get-tuple-element.14) | copy-start | bytes 221188
  139.7 79.2 %copy-start.10 = (f32[128]{0:T(128)S(1)}, f32[128]{0:T(128)}, u32[]{:S(2)}) copy-start(f32[128]{0:T(128)} %get-tuple-element.18) | copy-start | bytes 1540
Sparse Core Ops, SparseCore 0:
  32.5 50.2 all-reduce.5
  91.8 50.7 reduce-scatter.1
